TPU v7x, 32 devices: a whole 2x2x4 slice. The times are simulated.
32 devices in a mesh: dp: 8 (over z, y), tensor: 4 (over x, core).
Axes of the slice: x: 2, y: 2, z: 4, core: 2. Of those that a mesh axis runs over, the one named last changes fastest.
Arguments:
- hidden_in: bfloat16 [4096, 1024], P(('dp', 'tensor')), may hold values from -6 to 6
- cotangent: bfloat16 [4096, 1024], P(('dp', 'tensor')), may hold values from -6 to 6
- segment_ids: int32 [8, 512], P('dp'), may hold values from 0 to 3, never falling along the last dimension, each value on 1 to 256 neighbouring positions
- live_count: int32 [8], P('dp'), may hold values from 256 to 512, as said below
- first_gain: bfloat16 [1024], P(('dp', 'tensor')), may hold values from 0.25 to 1.75
- first_bias: bfloat16 [1024], P(('dp', 'tensor')), may hold values from -3 to 3
- second_gain: bfloat16 [1024], P(('dp', 'tensor')), may hold values from 0.25 to 1.75
- second_bias: bfloat16 [1024], P(('dp', 'tensor')), may hold values from -3 to 3
- attend_weight: bfloat16 [1024, 3, 1024], P('dp', None, 'tensor'), may hold values from -0.1875 to 0.1875
- attend_bias: bfloat16 [3, 1024], P(None, ('tensor', 'dp')), may hold values from -3 to 3
- output_weight: bfloat16 [1024, 1024], P('tensor', 'dp'), may hold values from -0.75 to 0.75
- output_bias: bfloat16 [1024], P(('dp', 'tensor')), may hold values from -3 to 3
- expand_weight: bfloat16 [1024, 4096], P('dp', 'tensor'), may hold values from -0.1875 to 0.1875
- expand_bias: bfloat16 [4096], P(('tensor', 'dp')), may hold values from -3 to 3
- shrink_weight: bfloat16 [4096, 1024], P('tensor', 'dp'), may hold values from -0.09375 to 0.09375
- shrink_bias: bfloat16 [1024], P(('dp', 'tensor')), may hold values from -3 to 3
Outputs:
- hidden_out: bfloat16 [4096, 1024], P(('dp', 'tensor'))
- input_grad: float32 [4096, 1024], P(('dp', 'tensor'))
- first_gain_grad: float32 [1024], P(('dp', 'tensor'))
- first_bias_grad: float32 [1024], P(('dp', 'tensor'))
- second_gain_grad: float32 [1024], P(('dp', 'tensor'))
- second_bias_grad: float32 [1024], P(('dp', 'tensor'))
- attend_weight_grad: float32 [1024, 3, 1024], P('dp', None, 'tensor')
- attend_bias_grad: float32 [3, 1024], P(None, ('tensor', 'dp'))
- output_weight_grad: float32 [1024, 1024], P('tensor', 'dp')
- output_bias_grad: float32 [1024], P(('dp', 'tensor'))
- expand_weight_grad: float32 [1024, 4096], P('dp', 'tensor')
- expand_bias_grad: float32 [4096], P(('tensor', 'dp'))
- shrink_weight_grad: float32 [4096, 1024], P('tensor', 'dp')
- shrink_bias_grad: float32 [1024], P(('dp', 'tensor'))
Inputs may be any that keep to these rules, and one draw needn't show every extreme that they name: `segment_ids`: in each group the segment ids never fall; each sequence has 1 to 256 tokens, and one has exactly 256. `live_count`: some group has all 512 tokens live.
All inputs are finite; a program needn't handle non-finite values.
Results may differ from a plain program's by a relative error of at most 0.012.
Values may be sent and summed in bfloat16 or wider, within the bound.
No kernel may reach another device: no remote copies, remote signals or barrier semaphores. Data moves between devices by JAX's collectives and lax.ppermute only.
A program may use at most 128 MiB of HBM per device.

v0:
```python
import jax
import jax.numpy as jnp
from jax import lax
from jax.sharding import PartitionSpec as P

HD = 64
ROT = 16


EPSILON = 1e-05
NEGATIVE = -1000000000.0


def rotate(tensor, cos_table, sin_table, rot_dims):
    half_dims = rot_dims // 2
    lower_half = tensor[..., :half_dims]
    upper_half = tensor[..., half_dims:rot_dims]
    return jnp.concatenate(
        [
            lower_half * cos_table - upper_half * sin_table,
            upper_half * cos_table + lower_half * sin_table,
            tensor[..., rot_dims:],
        ],
        axis=-1,
    )


def norm_backward(scaled, standard, inverse_std):
    mean_scaled = jnp.mean(scaled, axis=-1, keepdims=True)
    mean_cross = jnp.mean(scaled * standard, axis=-1, keepdims=True)
    return inverse_std * (scaled - mean_scaled - standard * mean_cross)


def per_device(
    hidden_in,
    cotangent,
    segment_ids,
    live_count,
    first_gain,
    first_bias,
    second_gain,
    second_bias,
    attend_weight,
    attend_bias,
    output_weight,
    output_bias,
    expand_weight,
    expand_bias,
    shrink_weight,
    shrink_bias,
):
    f32 = jnp.float32
    bf16 = jnp.bfloat16
    rows_all = lax.all_gather(hidden_in, "tensor", axis=0, tiled=True)
    vectors = (
        lax.all_gather(first_gain, ("dp", "tensor"), axis=0, tiled=True),
        lax.all_gather(first_bias, ("dp", "tensor"), axis=0, tiled=True),
        lax.all_gather(second_gain, ("dp", "tensor"), axis=0, tiled=True),
        lax.all_gather(second_bias, ("dp", "tensor"), axis=0, tiled=True),
        lax.all_gather(output_bias, ("dp", "tensor"), axis=0, tiled=True),
        lax.all_gather(shrink_bias, ("dp", "tensor"), axis=0, tiled=True),
    )
    gain_one, bias_one, gain_two, bias_two, out_bias_full, shrink_bias_full = [
        item.astype(f32) for item in vectors
    ]
    attend_full, output_full, expand_full, shrink_full, attend_bias_full, expand_bias_full = (
        lax.all_gather(attend_weight, "dp", axis=0, tiled=True),
        lax.all_gather(output_weight, "dp", axis=1, tiled=True),
        lax.all_gather(expand_weight, "dp", axis=0, tiled=True),
        lax.all_gather(shrink_weight, "dp", axis=1, tiled=True),
        lax.all_gather(attend_bias, "dp", axis=1, tiled=True),
        lax.all_gather(expand_bias, "dp", axis=0, tiled=True),
    )
    group_rows = rows_all.shape[0]
    local_heads = attend_full.shape[2] // HD
    scale = HD ** (-0.5)
    rows_float = rows_all.astype(f32)
    centre = rows_float - jnp.mean(rows_float, axis=-1, keepdims=True)
    inverse_std = lax.rsqrt(jnp.mean(centre * centre, axis=-1, keepdims=True) + EPSILON)
    standard = centre * inverse_std
    branch_one = (standard * gain_one + bias_one).astype(bf16)
    branch_two = (standard * gain_two + bias_two).astype(bf16)
    projected = (
        jnp.einsum("td,dcn->tcn", branch_one, attend_full, preferred_element_type=f32)
        + attend_bias_full.astype(f32)[None]
    )
    segments = segment_ids[0]
    index = jnp.arange(group_rows)
    same_seq = segments[:, None] == segments[None, :]
    positions = jnp.sum((same_seq & (index[None, :] < index[:, None])).astype(f32), axis=1)
    allowed = (
        same_seq
        & (index[None, :] <= index[:, None])
        & ((index[None, :] < live_count[0]) | (index[None, :] == index[:, None]))
    )
    half_dims = ROT // 2
    inverse = 10000.0 ** (-jnp.arange(half_dims).astype(f32) * 2.0 / ROT)
    angles = positions[:, None] * inverse[None, :]
    cos_table = jnp.cos(angles)[:, None, :]
    sin_table = jnp.sin(angles)[:, None, :]
    per_head = projected.reshape(group_rows, 3, local_heads, HD)
    queries = rotate(per_head[:, 0], cos_table, sin_table, ROT).astype(bf16)
    keys_rot = rotate(per_head[:, 1], cos_table, sin_table, ROT).astype(bf16)
    values = per_head[:, 2].astype(bf16)
    scores = jnp.einsum("thd,uhd->htu", queries, keys_rot, preferred_element_type=f32) * scale
    scores = jnp.where(allowed[None], scores, NEGATIVE)
    top_score = jnp.max(scores, axis=-1, keepdims=True)
    log_total = top_score + jnp.log(jnp.sum(jnp.exp(scores - top_score), axis=-1, keepdims=True))
    probs = jnp.exp(scores - log_total)
    mixed = jnp.einsum("htu,uhd->thd", probs.astype(bf16), values, preferred_element_type=f32)
    mixed = mixed.reshape(group_rows, local_heads * HD).astype(bf16)
    partial_out = jnp.dot(mixed, output_full, preferred_element_type=f32)
    expanded = jnp.dot(
        branch_two, expand_full, preferred_element_type=f32
    ) + expand_bias_full.astype(f32)
    activated, gelu_back = jax.vjp(lambda value: jax.nn.gelu(value, approximate=False), expanded)
    activated_low = activated.astype(bf16)
    partial_out = partial_out + jnp.dot(activated_low, shrink_full, preferred_element_type=f32)
    summed = lax.psum_scatter(
        partial_out.astype(jnp.bfloat16), "tensor", scatter_dimension=0, tiled=True
    ).astype(jnp.float32)
    hidden_out = (hidden_in.astype(f32) + summed + out_bias_full + shrink_bias_full).astype(bf16)
    attend_back, output_back, expand_back, shrink_back = (
        lax.all_gather(attend_weight, "dp", axis=0, tiled=True),
        lax.all_gather(output_weight, "dp", axis=1, tiled=True),
        lax.all_gather(expand_weight, "dp", axis=0, tiled=True),
        lax.all_gather(shrink_weight, "dp", axis=1, tiled=True),
    )
    grad_rows = lax.all_gather(cotangent, "tensor", axis=0, tiled=True)
    grad_local = cotangent.astype(f32)
    bias_sum = jnp.sum(grad_local, axis=0)
    grad_activated = jnp.einsum("te,fe->tf", grad_rows, shrink_back, preferred_element_type=f32)
    shrink_grad = jnp.einsum("tf,te->fe", activated_low, grad_rows, preferred_element_type=f32)
    grad_expanded = gelu_back(grad_activated)[0].astype(bf16)
    expand_bias_grad = jnp.sum(grad_expanded.astype(f32), axis=0)
    expand_grad = jnp.einsum("td,tf->df", branch_two, grad_expanded, preferred_element_type=f32)
    grad_two = jnp.einsum("tf,df->td", grad_expanded, expand_back, preferred_element_type=f32)
    grad_mixed = jnp.einsum("te,ne->tn", grad_rows, output_back, preferred_element_type=f32).astype(
        bf16
    )
    output_grad = jnp.einsum("tn,te->ne", mixed, grad_rows, preferred_element_type=f32)
    grad_mixed = grad_mixed.reshape(group_rows, local_heads, HD)
    scores_again = jnp.einsum("thd,uhd->htu", queries, keys_rot, preferred_element_type=f32) * scale
    probs_again = jnp.where(allowed[None], jnp.exp(scores_again - log_total), 0.0)
    grad_values = jnp.einsum(
        "htu,thd->uhd", probs_again.astype(bf16), grad_mixed, preferred_element_type=f32
    )
    grad_probs = jnp.einsum("thd,uhd->htu", grad_mixed, values, preferred_element_type=f32)
    row_cross = jnp.sum(grad_probs * probs_again, axis=-1, keepdims=True)
    grad_scores = (probs_again * (grad_probs - row_cross)).astype(bf16)
    grad_queries = (
        jnp.einsum("htu,uhd->thd", grad_scores, keys_rot, preferred_element_type=f32) * scale
    )
    grad_keys = jnp.einsum("htu,thd->uhd", grad_scores, queries, preferred_element_type=f32) * scale
    grad_projected = jnp.stack(
        [
            rotate(grad_queries, cos_table, -sin_table, ROT),
            rotate(grad_keys, cos_table, -sin_table, ROT),
            grad_values,
        ],
        axis=1,
    )
    grad_projected = grad_projected.reshape(group_rows, 3, local_heads * HD).astype(bf16)
    attend_bias_grad = jnp.sum(grad_projected.astype(f32), axis=0)
    attend_grad = jnp.einsum("td,tcn->dcn", branch_one, grad_projected, preferred_element_type=f32)
    grad_one = jnp.einsum("tcn,dcn->td", grad_projected, attend_back, preferred_element_type=f32)
    (
        attend_weight_grad,
        output_weight_grad,
        expand_weight_grad,
        shrink_weight_grad,
        attend_bias_out,
        expand_bias_out,
    ) = (
        lax.psum_scatter(attend_grad, "dp", scatter_dimension=0, tiled=True),
        lax.psum_scatter(output_grad, "dp", scatter_dimension=1, tiled=True),
        lax.psum_scatter(expand_grad, "dp", scatter_dimension=0, tiled=True),
        lax.psum_scatter(shrink_grad, "dp", scatter_dimension=1, tiled=True),
        lax.psum_scatter(attend_bias_grad, "dp", scatter_dimension=1, tiled=True),
        lax.psum_scatter(expand_bias_grad, "dp", scatter_dimension=0, tiled=True),
    )
    grad_one_local, grad_two_local = (
        lax.psum_scatter(
            grad_one.astype(jnp.bfloat16), "tensor", scatter_dimension=0, tiled=True
        ).astype(jnp.float32),
        lax.psum_scatter(
            grad_two.astype(jnp.bfloat16), "tensor", scatter_dimension=0, tiled=True
        ).astype(jnp.float32),
    )
    local_rows = hidden_in.shape[0]
    start = lax.axis_index("tensor") * local_rows
    standard_local = lax.dynamic_slice_in_dim(standard, start, local_rows, 0)
    inverse_local = lax.dynamic_slice_in_dim(inverse_std, start, local_rows, 0)
    scaled = grad_one_local * gain_one + grad_two_local * gain_two
    input_grad = grad_local + norm_backward(scaled, standard_local, inverse_local)
    gain_one_grad = jnp.sum(grad_one_local * standard_local, axis=0)
    bias_one_grad = jnp.sum(grad_one_local, axis=0)
    gain_two_grad = jnp.sum(grad_two_local * standard_local, axis=0)
    bias_two_grad = jnp.sum(grad_two_local, axis=0)
    first_gain_grad, first_bias_grad, second_gain_grad, second_bias_grad, out_bias_grad = (
        lax.psum_scatter(gain_one_grad, ("dp", "tensor"), scatter_dimension=0, tiled=True),
        lax.psum_scatter(bias_one_grad, ("dp", "tensor"), scatter_dimension=0, tiled=True),
        lax.psum_scatter(gain_two_grad, ("dp", "tensor"), scatter_dimension=0, tiled=True),
        lax.psum_scatter(bias_two_grad, ("dp", "tensor"), scatter_dimension=0, tiled=True),
        lax.psum_scatter(bias_sum, ("dp", "tensor"), scatter_dimension=0, tiled=True),
    )
    return (
        hidden_out,
        input_grad,
        first_gain_grad,
        first_bias_grad,
        second_gain_grad,
        second_bias_grad,
        attend_weight_grad,
        attend_bias_out,
        output_weight_grad,
        out_bias_grad,
        expand_weight_grad,
        expand_bias_out,
        shrink_weight_grad,
        out_bias_grad,
    )


def solution(mesh):
    in_specs = (
        P(("dp", "tensor"), None),
        P(("dp", "tensor"), None),
        P("dp", None),
        P("dp"),
        P(("dp", "tensor")),
        P(("dp", "tensor")),
        P(("dp", "tensor")),
        P(("dp", "tensor")),
        P("dp", None, "tensor"),
        P(None, ("tensor", "dp")),
        P("tensor", "dp"),
        P(("dp", "tensor")),
        P("dp", "tensor"),
        P(("tensor", "dp")),
        P("tensor", "dp"),
        P(("dp", "tensor")),
    )
    out_specs = (
        P(("dp", "tensor"), None),
        P(("dp", "tensor"), None),
        P(("dp", "tensor")),
        P(("dp", "tensor")),
        P(("dp", "tensor")),
        P(("dp", "tensor")),
        P("dp", None, "tensor"),
        P(None, ("tensor", "dp")),
        P("tensor", "dp"),
        P(("dp", "tensor")),
        P("dp", "tensor"),
        P(("tensor", "dp")),
        P("tensor", "dp"),
        P(("dp", "tensor")),
    )
    return jax.shard_map(
        per_device, mesh=mesh, in_specs=in_specs, out_specs=out_specs, check_vma=False
    )
```

profile of v0, /device:TPU:0, one launch (start us, length us, event | category | flops | bytes accessed | tf_op | source)
XLA Modules:
  0.0 681.0 jit_solution(17750717601277931043)
XLA Ops:
  7.2 0.7 all-gather.8.cloned.1.call-update
  8.0 0.7 all-gather.16.cloned.1.call-update
  8.7 1.7 copy.62
  12.4 0.9 convert_reduce_fusion.3
  13.3 0.8 dynamic-update-slice.5
  14.2 0.8 dynamic-update-slice
  15.0 0.8 dynamic-update-slice.1
  15.9 0.8 dynamic-update-slice.2
  16.7 0.8 dynamic-update-slice.3
  17.5 0.8 dynamic-update-slice.4
  18.4 42.2 %all-reduce.13 = (bf16[1024]{0:T(1024)(128)(2,1)S(1)}, bf16[1024]{0:T(1024)(128)(2,1)S(1)}, bf16[1024]{0:T(1024)(128)(2,1)S(1)}, bf16[1024]{0:T(1024)(128)(2,1)S...) all-reduce(bf16[1024]{0:T(1024)(128)(2,1)S(1)} %dynamic-update-slic, ...), channel_id=1, replica_groups=mesh['dp'=8,'tensor'=4] {'dp','tensor'}, use_global_device_ids=true, to_apply=%add.3 | all-reduce | flops 6144 | bytes 24576
  60.6 0.6 convert_element_type.124
  61.2 0.6 convert_element_type.123
  61.8 20.9 %all-gather.1 = bf16[8,1,128]{2,1,0:T(2,128)(2,1)S(1)} all-gather(bf16[1,1,128]{2,1,0:T(2,128)(2,1)} %bitcast.85), channel_id=1, replica_groups=mesh['dp'=8,'tensor'=4] {'dp'}, dimensions={0}, use_global_device_ids=true | all-gather | bytes 2304 | tf_op jit(solution)/shard_map/all_gather | solution.py:72
  82.7 0.6 convert_element_type.145
  83.3 16.8 %all-gather = bf16[8,32,3]{1,2,0:T(4,128)(2,1)S(1)} all-gather(bf16[1,32,3]{1,2,0:T(4,128)(2,1)} %bitcast.84), channel_id=1, replica_groups=mesh['dp'=8,'tensor'=4] {'dp'}, dimensions={0}, use_global_device_ids=true | all-gather | bytes 1728 | tf_op jit(solution)/shard_map/all_gather | solution.py:71
  100.1 1.0 fusion.23
  101.1 29.7 %all_gather.51 = bf16[256,1024]{1,0:T(8,128)(2,1)S(1)} all-gather(bf16[256,128]{1,0:T(8,128)(2,1)S(1)} %copy-done.24), channel_id=1, replica_groups=mesh['dp'=8,'tensor'=4] {'dp'}, dimensions={1}, use_global_device_ids=true | all-gather | bytes 589824 | tf_op jit(solution)/shard_map/all_gather | solution.py:68
  130.9 0.8 fusion.39
  131.6 1.5 convert_reduce_fusion
  133.2 1.6 fusion.4
  134.9 2.4 convolution_convert_fusion.1
  137.3 2.6 convolution_add_fusion
  140.7 0.9 fusion
  141.7 0.9 exponential_reduce_fusion
  142.7 1.0 copy-done
  143.6 1.7 fusion.19
  145.4 1.1 copy.70
  146.5 3.8 multiply_reduce_fusion
  150.4 1.3 multiply_convert_fusion
  151.7 0.8 fusion.16
  153.7 0.8 copy.80
  154.6 3.4 bitcast_convert_fusion
  158.4 4.3 fusion.30
  162.7 36.1 %all-gather.14.cloned.1.call-done = bf16[1024,1024]{1,0:T(8,128)(2,1)} async-done(((bf16[1024,128]{1,0:T(8,128)(2,1)}), bf16[1024,1024]{1,0:T(8,128)(2,1)}) %all-gather.14.cloned.1.call-update) | async-done | bytes 2097168 | tf_op jit(solution)/shard_map/all_gather | solution.py:70
  198.8 8.8 %convert_reduce_fusion.1 = (f32[1024]{0:T(1024)S(1)}, bf16[512,1024]{1,0:T(8,128)(2,1)S(1)}, f32[512,1024]{1,0:T(8,128)}) fusion(f32[512,1024]{1,0:T(8,128)} %fusion.30, f32[1024]{0:T(1024)S(1)} %bitcast.81, bf16[512,1024]{1,0:T(8,128)(2,1)S(1)} %copy-done.3, bf16[1024,1024]{1,0:T(8,128)(2,1)} %all-gather.14.cloned.1.call-done), kind=kOutput, calls=%fused_computation.16 | convolution fusion | flops 1113062400 | bytes 8396800 | tf_op jit(solution)/shard_map/te,fe->tf/dot_general | solution.py:132
  207.6 1.0 copy-done.44
  208.6 2.3 convolution_convert_fusion
  211.0 3.7 fusion.18
  215.3 1.1 copy-done.40
  216.4 1.3 fusion.52
  217.7 1.5 add_convert_fusion.1
  219.2 2.4 fusion.53
  221.8 3.9 fusion.36
  225.8 3.2 fusion.54
  229.4 0.9 copy-done.45
  230.3 3.4 fusion.29
  233.7 0.6 copy-done.42
  234.3 0.6 dynamic-slice.9
  236.0 26.0 %reduce-scatter.25.cloned.1.call-done = f32[32,3]{1,0:T(8,128)} async-done(((f32[256,3]{1,0:T(8,128)}), f32[32,3]{1,0:T(8,128)}) %reduce-scatter.25.cloned.1.call-update) | async-done | bytes 400
  262.0 1.4 copy.81
  263.4 19.5 %all-reduce.11 = f32[1024]{0:T(1024)S(1)} all-reduce(f32[1024]{0:T(1024)S(1)} %get-tuple-element.31), channel_id=14, replica_groups=mesh['dp'=8,'tensor'=4] {'dp'}, use_global_device_ids=true, to_apply=%region_27.28.clone | all-reduce | flops 1024 | bytes 8192
  282.9 0.6 dynamic-slice.10
  283.5 4.9 reduce-scatter.13.cloned.1.call-done
  288.4 27.4 %reduce-scatter.15.cloned.1.call-done = bf16[128,1024]{1,0:T(8,128)(2,1)} async-done(((bf16[512,1024]{1,0:T(8,128)(2,1)}), bf16[128,1024]{1,0:T(8,128)(2,1)}) %reduce-scatter.15.cloned.1.call-update) | async-done | bytes 262160 | tf_op jit(solution)/shard_map/reduce_scatter | solution.py:186
  315.8 1.4 fusion.27
  317.2 2.1 convert_reduce_fusion.6
  319.2 39.6 %all-reduce.12 = (f32[1024]{0:T(1024)S(1)}, f32[1024]{0:T(1024)S(1)}, f32[1024]{0:T(1024)S(1)}, f32[1024]{0:T(1024)S(1)}, f32[1024]{0:T(1024)S(1)}) all-reduce(f32[1024]{0:T(1024)S(1)} %get-tuple-element.16, f32[1024]{0:T(1024)S(1)} %get-tuple-element.18, ...), channel_id=5, replica_groups=mesh['dp'=8,'tensor'=4] {'dp','tensor'}, use_global_device_ids=true, to_apply=%region_12.13.clone | all-reduce | flops 5120 | bytes 40960
  358.8 0.6 dynamic-slice.4
  361.3 1.8 add_convert_fusion.4
  363.0 49.0 %reduce-scatter.19.cloned.1.call-done = f32[256,128]{1,0:T(8,128)} async-done(((f32[256,1024]{1,0:T(8,128)}), f32[256,128]{1,0:T(8,128)}) %reduce-scatter.19.cloned.1.call-update) | async-done | bytes 131088 | tf_op jit(solution)/shard_map/reduce_scatter | solution.py:176
  412.0 77.9 %reduce-scatter.17.cloned.1.call-done = f32[128,3,256]{2,0,1:T(8,128)} async-done(((f32[1024,3,256]{2,0,1:T(8,128)}), f32[128,3,256]{2,0,1:T(8,128)}) %reduce-scatter.17.cloned.1.call-update) | async-done | bytes 393232 | tf_op jit(solution)/shard_map/reduce_scatter | solution.py:175
  489.9 91.9 %reduce-scatter.23.cloned.1.call-done = f32[1024,128]{1,0:T(8,128)} async-done(((f32[1024,1024]{1,0:T(8,128)}), f32[1024,128]{1,0:T(8,128)}) %reduce-scatter.23.cloned.1.call-update) | async-done | bytes 524304 | tf_op jit(solution)/shard_map/reduce_scatter | solution.py:178
  581.8 92.2 %reduce-scatter.21.cloned.1.call-done = f32[128,1024]{1,0:T(8,128)} async-done(((f32[1024,1024]{1,0:T(8,128)}), f32[128,1024]{1,0:T(8,128)}) %reduce-scatter.21.cloned.1.call-update) | async-done | bytes 524304 | tf_op jit(solution)/shard_map/reduce_scatter | solution.py:177
  (155 shorter events, 7.7 us)
Async XLA Ops:
  7.2 94.0 %copy-start.24 = (bf16[256,128]{1,0:T(8,128)(2,1)S(1)}, bf16[256,128]{1,0:T(8,128)(2,1)}, u32[]{:S(2)}) copy-start(bf16[256,128]{1,0:T(8,128)(2,1)} %param.26) | copy-start | bytes 196612
  7.2 124.5 %all-gather.8.cloned.1.call-start = ((), (), s32[]{:S(2)}) async-start(), calls=%async_computation.8 | async-start | bytes 1310720 | tf_op jit(solution)/shard_map/all_gather | solution.py:54
  7.9 126.9 %all-gather.16.cloned.1.call-start = ((), (), s32[]{:S(2)}) async-start(), calls=%async_computation.13 | async-start | bytes 1310720 | tf_op jit(solution)/shard_map/all_gather | solution.py:129
  8.7 128.6 %all-gather.10.cloned.1.call-start = ((), (), s32[]{:S(2)}) async-start(), calls=%async_computation.9 | async-start | bytes 1769472 | tf_op jit(solution)/shard_map/all_gather | solution.py:67
  10.5 147.9 %all-gather.12.cloned.1.call-start = ((), (), s32[]{:S(2)}) async-start(), calls=%async_computation.10 | async-start | bytes 2359296 | tf_op jit(solution)/shard_map/all_gather | solution.py:69
  11.1 187.7 %all-gather.14.cloned.1.call-start = ((), (), s32[]{:S(2)}) async-start(), calls=%async_computation.11 | async-start | bytes 2359296 | tf_op jit(solution)/shard_map/all_gather | solution.py:70
  11.7 250.4 %reduce-scatter.25.cloned.1.call-start = ((), (), s32[]{:S(2)}) async-start(), calls=%async_computation.20 | async-start | bytes 147456
  61.8 75.5 %copy-start.28 = (f32[1024]{0:T(1024)}, f32[1024]{0:T(1024)S(1)}, u32[]{:S(2)}) copy-start(f32[1024]{0:T(1024)S(1)} %convert_element_type.112) | copy-start | bytes 12292
  61.8 75.5 %copy-start.36 = (f32[1024]{0:T(1024)}, f32[1024]{0:T(1024)S(1)}, u32[]{:S(2)}) copy-start(f32[1024]{0:T(1024)S(1)} %convert_element_type.113) | copy-start | bytes 12292
  130.9 9.1 %copy-start.4 = (bf16[256,1024]{1,0:T(8,128)(2,1)}, bf16[256,1024]{1,0:T(8,128)(2,1)S(1)}, u32[]{:S(2)}) copy-start(bf16[256,1024]{1,0:T(8,128)(2,1)S(1)} %all_gather.51) | copy-start | bytes 1572868
  131.6 5.7 copy-start.2
  133.2 6.8 copy-start.30
  134.8 5.1 copy-start.33
  140.0 6.5 copy-start.8
  140.0 0.7 copy-start.26
  140.1 1.6 copy-start.16
  140.1 1.5 copy-start.18
  141.7 2.0 copy-start
  141.7 1.9 copy-start.20
  142.7 2.7 copy-start.21
  146.5 8.1 %copy-start.10 = (bf16[512,1,256]{2,0,1:T(8,128)(2,1)}, bf16[512,1,256]{2,0,1:T(8,128)(2,1)S(1)}, u32[]{:S(2)}) copy-start(bf16[512,1,256]{2,0,1:T(8,128)(2,1)S(1)} %copy.70) | copy-start | bytes 786436
  146.5 3.8 copy-start.1
  146.5 3.8 copy-start.22
  150.4 1.3 copy-start.19
  151.7 0.9 copy-start.17
  152.4 0.7 copy-start.25
  153.4 4.6 copy-start.12
  153.6 4.5 copy-start.13
  154.5 3.9 copy-start.27
  154.5 3.9 copy-start.31
  154.5 3.9 copy-start.34
  154.5 3.9 copy-start.35
  154.6 133.8 %reduce-scatter.13.cloned.1.call-start = ((), (), s32[]{:S(2)}) async-start(), calls=%async_computation.14 | async-start | bytes 1310720 | tf_op jit(solution)/shard_map/reduce_scatter | solution.py:183
  158.1 40.7 %copy-start.3 = (bf16[512,1024]{1,0:T(8,128)(2,1)S(1)}, bf16[512,1024]{1,0:T(8,128)(2,1)}, u32[]{:S(2)}) copy-start(bf16[512,1024]{1,0:T(8,128)(2,1)} %all-gather.16.cloned.1.call-done) | copy-start | bytes 3145732
  158.1 40.7 %copy-start.32 = (f32[8,1,128]{2,1,0:T(1,128)S(1)}, f32[8,1,128]{2,1,0:T(1,128)}, u32[]{:S(2)}) copy-start(f32[8,1,128]{2,1,0:T(1,128)} %convert_element_type.145) | copy-start | bytes 12292
  158.1 157.7 %reduce-scatter.15.cloned.1.call-start = ((), (), s32[]{:S(2)}) async-start(), calls=%async_computation.15 | async-start | bytes 1310720 | tf_op jit(solution)/shard_map/reduce_scatter | solution.py:186
  198.8 9.8 %copy-start.41 = (bf16[1024,1024]{1,0:T(8,128)(2,1)S(1)}, bf16[1024,1024]{1,0:T(8,128)(2,1)}, u32[]{:S(2)}) copy-start(bf16[1024,1024]{1,0:T(8,128)(2,1)} %all-gather.12.cloned.1.call-done) | copy-start | bytes 6291460
  207.6 1.0 copy-start.44
  208.6 2.4 copy-start.23
  210.9 150.3 %reduce-scatter.11.cloned.1.call-start = ((), (), s32[]{:S(2)}) async-start(), calls=%async_computation.12 | async-start | bytes 1310720 | tf_op jit(solution)/shard_map/reduce_scatter | solution.py:119
  211.0 3.7 copy-start.6
  211.0 3.7 copy-start.7
  214.7 3.0 copy-start.15
  214.7 1.7 copy-start.40
  216.4 1.3 copy-start.5
  219.2 2.6 copy-start.11
  219.2 2.6 copy-start.29
  219.2 2.6 copy-start.37
  219.2 192.8 %reduce-scatter.19.cloned.1.call-start = ((), (), s32[]{:S(2)}) async-start(), calls=%async_computation.17 | async-start | bytes 1179648 | tf_op jit(solution)/shard_map/reduce_scatter | solution.py:176
  221.7 268.2 %reduce-scatter.17.cloned.1.call-start = ((), (), s32[]{:S(2)}) async-start(), calls=%async_computation.16 | async-start | bytes 3538944 | tf_op jit(solution)/shard_map/reduce_scatter | solution.py:175
  225.7 356.1 %reduce-scatter.23.cloned.1.call-start = ((), (), s32[]{:S(2)}) async-start(), calls=%async_computation.19 | async-start | bytes 4718592 | tf_op jit(solution)/shard_map/reduce_scatter | solution.py:178
  229.0 1.2 copy-start.45
  229.1 444.9 %reduce-scatter.21.cloned.1.call-start = ((), (), s32[]{:S(2)}) async-start(), calls=%async_computation.18 | async-start | bytes 4718592 | tf_op jit(solution)/shard_map/reduce_scatter | solution.py:177
  233.7 0.7 copy-start.42
  233.7 1.2 copy-start.39
  233.7 1.2 copy-start.38
  235.7 81.5 %copy-start.14 = (bf16[128,1024]{1,0:T(8,128)(2,1)S(1)}, bf16[128,1024]{1,0:T(8,128)(2,1)}, u32[]{:S(2)}) copy-start(bf16[128,1024]{1,0:T(8,128)(2,1)} %param.17) | copy-start | bytes 786436
  236.0 125.3 %copy-start.9 = (bf16[128,1024]{1,0:T(8,128)(2,1)S(1)}, bf16[128,1024]{1,0:T(8,128)(2,1)}, u32[]{:S(2)}) copy-start(bf16[128,1024]{1,0:T(8,128)(2,1)} %param.16) | copy-start | bytes 786436
  359.5 315.0 %copy-start.43 = (f32[32]{0:T(128)}, f32[32]{0:T(128)S(1)}, u32[]{:S(2)}) copy-start(f32[32]{0:T(128)S(1)} %dynamic-slice.8) | copy-start | bytes 388
Sparse Core Ops, SparseCore 0:
  9.6 19.6 all-gather.7
  30.8 17.0 all-gather.15
  50.5 44.5 all-gather.9
  97.0 51.4 all-gather.11
  150.3 48.4 all-gather.13
  202.0 60.0 reduce-scatter.24
  264.5 23.7 reduce-scatter.12
  290.9 24.8 reduce-scatter.14
  318.3 24.8 reduce-scatter.10
  347.0 64.9 reduce-scatter.18
  416.2 73.6 reduce-scatter.16
  493.9 87.8 reduce-scatter.22
  586.0 87.9 reduce-scatter.20
where the time goes:
time: 682 us; the launch traced here: 681 us
  waiting for transfers between devices  408 us (60%)
  blocking collectives  169 us (25%)
  matrix products  51 us (7%)
  local copies, waits for them, and re-layouts  20.3 us (3%)
  other arithmetic  16.2 us (2%)
  between operations  15.9 us (2%)
    unnamed x3, blocking collectives  101 us
    reduce_scatter x1, waiting for transfers between devices, per_device(): lax.psum_scatter(expand_grad, 'dp', scatter_dimension=0, tiled=True)  92.2 us
    reduce_scatter x1, waiting for transfers between devices, per_device(): lax.psum_scatter(shrink_grad, 'dp', scatter_dimension=1, tiled=True)  91.9 us
    reduce_scatter x1, waiting for transfers between devices, per_device(): lax.psum_scatter(attend_grad, 'dp', scatter_dimension=0, tiled=True)  77.9 us
    reduce_scatter x1, waiting for transfers between devices, per_device(): lax.psum_scatter(output_grad, 'dp', scatter_dimension=1, tiled=True)  49 us
    all_gather x1, waiting for transfers between devices, per_device(): lax.all_gather(shrink_weight, 'dp', axis=1, tiled=True)  36.1 us
    all_gather x1, blocking collectives, per_device(): lax.all_gather(output_weight, 'dp', axis=1, tiled=True)  29.7 us
    unnamed x14, waiting for transfers between devices  28.6 us
  transfers between devices with their start and end apart: 13, of which 8 were waited for; matrix products, arithmetic and copies ran while one was open for 12% of the time, Pallas kernels for 0%

commit v1 on v0

v1 whole, which is shorter than its diff:
```python
import jax
import jax.numpy as jnp
from jax import lax
from jax.sharding import PartitionSpec as P

HD = 64
ROT = 16


EPSILON = 1e-05
NEGATIVE = -1000000000.0


def rotate(tensor, cos_table, sin_table, rot_dims):
    half_dims = rot_dims // 2
    lower_half = tensor[..., :half_dims]
    upper_half = tensor[..., half_dims:rot_dims]
    return jnp.concatenate(
        [
            lower_half * cos_table - upper_half * sin_table,
            upper_half * cos_table + lower_half * sin_table,
            tensor[..., rot_dims:],
        ],
        axis=-1,
    )


def norm_backward(scaled, standard, inverse_std):
    mean_scaled = jnp.mean(scaled, axis=-1, keepdims=True)
    mean_cross = jnp.mean(scaled * standard, axis=-1, keepdims=True)
    return inverse_std * (scaled - mean_scaled - standard * mean_cross)


def lane_rows(parts, axis=1):
    padded = []
    for part in parts:
        extra = -part.shape[1] % 128
        padded.append(jnp.pad(part, ((0, 0), (0, extra))))
    joined = jnp.concatenate(padded, axis=axis)
    joined = joined.reshape(joined.shape[0], -1, 128)
    joined = jnp.pad(joined, ((0, 0), (0, -joined.shape[1] % 16), (0, 0)))
    return joined.reshape(-1, 128)


def solution(mesh):
    dp_count = mesh.shape["dp"]
    tp_count = mesh.shape["tensor"]

    def per_device(
        hidden_in,
        cotangent,
        segment_ids,
        live_count,
        first_gain,
        first_bias,
        second_gain,
        second_bias,
        attend_weight,
        attend_bias,
        output_weight,
        output_bias,
        expand_weight,
        expand_bias,
        shrink_weight,
        shrink_bias,
    ):
        f32 = jnp.float32
        bf16 = jnp.bfloat16
        local_rows, width = hidden_in.shape
        group_rows = local_rows * tp_count
        piece = first_gain.shape[0]
        dp_rows, _, local_cols = attend_weight.shape
        local_ff = expand_weight.shape[1]
        tensor_index = lax.axis_index("tensor")

        small = jnp.concatenate(
            [
                first_gain,
                first_bias,
                second_gain,
                second_bias,
                output_bias,
                shrink_bias,
                attend_bias.reshape(-1),
                expand_bias,
            ]
        )
        small_len = small.shape[0]
        small_row = jnp.zeros((1, width), bf16).at[0, :small_len].set(small)
        gathered = lax.all_gather(
            jnp.concatenate([hidden_in, cotangent, small_row], axis=0), "tensor", axis=0
        )
        rows_all = gathered[:, :local_rows].reshape(group_rows, width)
        grad_rows = gathered[:, local_rows : 2 * local_rows].reshape(group_rows, width)
        small_tensor = gathered[:, 2 * local_rows, :small_len]

        ffn_sizes = (expand_weight.size, shrink_weight.size)
        ffn_all = lax.all_gather(
            jnp.concatenate(
                [expand_weight.reshape(-1), shrink_weight.reshape(-1), small_tensor.reshape(-1)]
            ),
            "dp",
            axis=0,
        )
        expand_full = ffn_all[:, : ffn_sizes[0]].reshape(dp_count * dp_rows, local_ff)
        shrink_parts = ffn_all[:, ffn_sizes[0] : ffn_sizes[0] + ffn_sizes[1]].reshape(
            dp_count, local_ff, dp_rows
        )
        small_all = ffn_all[:, ffn_sizes[0] + ffn_sizes[1] :].reshape(dp_count, tp_count, small_len)

        def full_vector(k):
            return small_all[:, :, k * piece : (k + 1) * piece].reshape(-1).astype(f32)

        gain_one, bias_one, gain_two, bias_two, out_bias_full, shrink_bias_full = [
            full_vector(k) for k in range(6)
        ]
        small_mine = lax.dynamic_index_in_dim(small_all, tensor_index, axis=1, keepdims=False)
        attend_bias_full = (
            small_mine[:, 6 * piece : 6 * piece + attend_bias.size]
            .reshape(dp_count, 3, attend_bias.shape[1])
            .transpose(1, 0, 2)
            .reshape(3, local_cols)
        )
        expand_bias_full = small_mine[:, 6 * piece + attend_bias.size :].reshape(-1)

        attend_all = lax.all_gather(
            jnp.concatenate([attend_weight.reshape(-1), output_weight.reshape(-1)]), "dp", axis=0
        )
        attend_full = attend_all[:, : attend_weight.size].reshape(dp_count * dp_rows, 3, local_cols)
        output_parts = attend_all[:, attend_weight.size :].reshape(dp_count, local_cols, dp_rows)

        local_heads = local_cols // HD
        scale = HD ** (-0.5)
        rows_float = rows_all.astype(f32)
        centre = rows_float - jnp.mean(rows_float, axis=-1, keepdims=True)
        inverse_std = lax.rsqrt(jnp.mean(centre * centre, axis=-1, keepdims=True) + EPSILON)
        standard = centre * inverse_std
        branch_one = (standard * gain_one + bias_one).astype(bf16)
        branch_two = (standard * gain_two + bias_two).astype(bf16)
        grad_rows_parts = grad_rows.reshape(group_rows, dp_count, dp_rows)

        expanded = jnp.dot(
            branch_two, expand_full, preferred_element_type=f32
        ) + expand_bias_full.astype(f32)
        activated, gelu_back = jax.vjp(lambda value: jax.nn.gelu(value, approximate=False), expanded)
        activated_low = activated.astype(bf16)
        ffn_out = jnp.einsum(
            "tf,kfe->tke", activated_low, shrink_parts, preferred_element_type=f32
        ).reshape(group_rows, width)
        grad_activated = jnp.einsum(
            "tke,kfe->tf", grad_rows_parts, shrink_parts, preferred_element_type=f32
        )
        shrink_grad = jnp.einsum(
            "tf,tke->kfe", activated_low, grad_rows_parts, preferred_element_type=f32
        )
        grad_expanded = gelu_back(grad_activated)[0].astype(bf16)
        expand_bias_grad = jnp.sum(grad_expanded.astype(f32), axis=0)
        expand_grad = jnp.einsum("td,tf->df", branch_two, grad_expanded, preferred_element_type=f32)
        grad_two = jnp.einsum("tf,df->td", grad_expanded, expand_full, preferred_element_type=f32)
        out_bias_sum = jnp.sum(grad_rows.astype(f32), axis=0).reshape(dp_count, tp_count, piece)
        out_bias_mine = lax.dynamic_index_in_dim(out_bias_sum, tensor_index, axis=1, keepdims=False)
        ffn_grads = lax.psum_scatter(
            lane_rows(
                [
                    expand_grad.reshape(dp_count, -1),
                    shrink_grad.reshape(dp_count, -1),
                    expand_bias_grad.reshape(dp_count, -1),
                    out_bias_mine,
                ],
                axis=1,
            ).astype(bf16),
            "dp",
            scatter_dimension=0,
            tiled=True,
        ).reshape(-1).astype(f32)
        at = 0
        expand_weight_grad = ffn_grads[at : at + expand_weight.size].reshape(expand_weight.shape)
        at += -(-expand_weight.size // 128) * 128
        shrink_weight_grad = ffn_grads[at : at + shrink_weight.size].reshape(shrink_weight.shape)
        at += -(-shrink_weight.size // 128) * 128
        expand_bias_out = ffn_grads[at : at + expand_bias.size]
        at += -(-expand_bias.size // 128) * 128
        out_bias_grad = ffn_grads[at : at + piece]

        projected = (
            jnp.einsum("td,dcn->tcn", branch_one, attend_full, preferred_element_type=f32)
            + attend_bias_full.astype(f32)[None]
        )
        segments = segment_ids[0]
        index = jnp.arange(group_rows)
        same_seq = segments[:, None] == segments[None, :]
        positions = jnp.sum((same_seq & (index[None, :] < index[:, None])).astype(f32), axis=1)
        allowed = (
            same_seq
            & (index[None, :] <= index[:, None])
            & ((index[None, :] < live_count[0]) | (index[None, :] == index[:, None]))
        )
        half_dims = ROT // 2
        inverse = 10000.0 ** (-jnp.arange(half_dims).astype(f32) * 2.0 / ROT)
        angles = positions[:, None] * inverse[None, :]
        cos_table = jnp.cos(angles)[:, None, :]
        sin_table = jnp.sin(angles)[:, None, :]
        per_head = projected.reshape(group_rows, 3, local_heads, HD)
        queries = rotate(per_head[:, 0], cos_table, sin_table, ROT).astype(bf16)
        keys_rot = rotate(per_head[:, 1], cos_table, sin_table, ROT).astype(bf16)
        values = per_head[:, 2].astype(bf16)
        scores = jnp.einsum("thd,uhd->htu", queries, keys_rot, preferred_element_type=f32) * scale
        scores = jnp.where(allowed[None], scores, NEGATIVE)
        top_score = jnp.max(scores, axis=-1, keepdims=True)
        log_total = top_score + jnp.log(jnp.sum(jnp.exp(scores - top_score), axis=-1, keepdims=True))
        probs = jnp.exp(scores - log_total)
        mixed = jnp.einsum("htu,uhd->thd", probs.astype(bf16), values, preferred_element_type=f32)
        mixed = mixed.reshape(group_rows, local_heads * HD).astype(bf16)
        partial_out = ffn_out + jnp.einsum(
            "tn,kne->tke", mixed, output_parts, preferred_element_type=f32
        ).reshape(group_rows, width)

        grad_mixed = jnp.einsum(
            "tke,kne->tn", grad_rows_parts, output_parts, preferred_element_type=f32
        ).astype(bf16)
        output_grad = jnp.einsum("tn,tke->kne", mixed, grad_rows_parts, preferred_element_type=f32)
        grad_mixed = grad_mixed.reshape(group_rows, local_heads, HD)
        probs_again = jnp.where(allowed[None], probs, 0.0)
        grad_values = jnp.einsum(
            "htu,thd->uhd", probs_again.astype(bf16), grad_mixed, preferred_element_type=f32
        )
        grad_probs = jnp.einsum("thd,uhd->htu", grad_mixed, values, preferred_element_type=f32)
        row_cross = jnp.sum(grad_probs * probs_again, axis=-1, keepdims=True)
        grad_scores = (probs_again * (grad_probs - row_cross)).astype(bf16)
        grad_queries = (
            jnp.einsum("htu,uhd->thd", grad_scores, keys_rot, preferred_element_type=f32) * scale
        )
        grad_keys = jnp.einsum("htu,thd->uhd", grad_scores, queries, preferred_element_type=f32) * scale
        grad_projected = jnp.stack(
            [
                rotate(grad_queries, cos_table, -sin_table, ROT),
                rotate(grad_keys, cos_table, -sin_table, ROT),
                grad_values,
            ],
            axis=1,
        )
        grad_projected = grad_projected.reshape(group_rows, 3, local_cols).astype(bf16)
        attend_bias_grad = jnp.sum(grad_projected.astype(f32), axis=0)
        attend_grad = jnp.einsum("td,tcn->dcn", branch_one, grad_projected, preferred_element_type=f32)
        grad_one = jnp.einsum("tcn,dcn->td", grad_projected, attend_full, preferred_element_type=f32)

        norm_partials = jnp.stack(
            [
                jnp.sum(grad_one * standard, axis=0),
                jnp.sum(grad_one, axis=0),
                jnp.sum(grad_two * standard, axis=0),
                jnp.sum(grad_two, axis=0),
            ]
        )
        norm_rows = (
            norm_partials.reshape(4, dp_count, tp_count, piece)
            .transpose(2, 0, 1, 3)
            .reshape(tp_count, 1, -1)
        )
        norm_len = norm_rows.shape[2]
        norm_rows = jnp.pad(norm_rows, ((0, 0), (0, 0), (0, 3 * width - norm_len)))
        token_parts = jnp.concatenate([partial_out, grad_one, grad_two], axis=1).reshape(
            tp_count, local_rows, 3 * width
        )
        reduced = lax.psum_scatter(
            jnp.concatenate([token_parts, norm_rows], axis=1).astype(bf16),
            "tensor",
            scatter_dimension=0,
        ).astype(f32)
        summed = reduced[:local_rows, :width]
        grad_one_local = reduced[:local_rows, width : 2 * width]
        grad_two_local = reduced[:local_rows, 2 * width :]
        norm_mine = reduced[local_rows, :norm_len].reshape(4, dp_count, piece).transpose(1, 0, 2)

        attend_bias_parts = (
            attend_bias_grad.reshape(3, dp_count, attend_bias.shape[1])
            .transpose(1, 0, 2)
            .reshape(dp_count, -1)
        )
        attn_grads = lax.psum_scatter(
            lane_rows(
                [
                    attend_grad.reshape(dp_count, -1),
                    output_grad.reshape(dp_count, -1),
                    attend_bias_parts,
                    norm_mine.reshape(dp_count, -1),
                ],
                axis=1,
            ).astype(bf16),
            "dp",
            scatter_dimension=0,
            tiled=True,
        ).reshape(-1).astype(f32)
        at = 0
        attend_weight_grad = attn_grads[at : at + attend_weight.size].reshape(attend_weight.shape)
        at += -(-attend_weight.size // 128) * 128
        output_weight_grad = attn_grads[at : at + output_weight.size].reshape(output_weight.shape)
        at += -(-output_weight.size // 128) * 128
        attend_bias_out = attn_grads[at : at + attend_bias.size].reshape(attend_bias.shape)
        at += -(-attend_bias.size // 128) * 128
        norm_grads = attn_grads[at : at + 4 * piece].reshape(4, piece)

        hidden_out = (hidden_in.astype(f32) + summed + out_bias_full + shrink_bias_full).astype(bf16)
        start = tensor_index * local_rows
        standard_local = lax.dynamic_slice_in_dim(standard, start, local_rows, 0)
        inverse_local = lax.dynamic_slice_in_dim(inverse_std, start, local_rows, 0)
        scaled = grad_one_local * gain_one + grad_two_local * gain_two
        input_grad = cotangent.astype(f32) + norm_backward(scaled, standard_local, inverse_local)
        return (
            hidden_out,
            input_grad,
            norm_grads[0],
            norm_grads[1],
            norm_grads[2],
            norm_grads[3],
            attend_weight_grad,
            attend_bias_out,
            output_weight_grad,
            out_bias_grad,
            expand_weight_grad,
            expand_bias_out,
            shrink_weight_grad,
            out_bias_grad,
        )
    in_specs = (
        P(("dp", "tensor"), None),
        P(("dp", "tensor"), None),
        P("dp", None),
        P("dp"),
        P(("dp", "tensor")),
        P(("dp", "tensor")),
        P(("dp", "tensor")),
        P(("dp", "tensor")),
        P("dp", None, "tensor"),
        P(None, ("tensor", "dp")),
        P("tensor", "dp"),
        P(("dp", "tensor")),
        P("dp", "tensor"),
        P(("tensor", "dp")),
        P("tensor", "dp"),
        P(("dp", "tensor")),
    )
    out_specs = (
        P(("dp", "tensor"), None),
        P(("dp", "tensor"), None),
        P(("dp", "tensor")),
        P(("dp", "tensor")),
        P(("dp", "tensor")),
        P(("dp", "tensor")),
        P("dp", None, "tensor"),
        P(None, ("tensor", "dp")),
        P("tensor", "dp"),
        P(("dp", "tensor")),
        P("dp", "tensor"),
        P(("tensor", "dp")),
        P("tensor", "dp"),
        P(("dp", "tensor")),
    )
    return jax.shard_map(
        per_device, mesh=mesh, in_specs=in_specs, out_specs=out_specs, check_vma=False
    )
```

time: 682 us -> 510 us (0.75); the launches traced: 681 us -> 502 us
  blocking collectives: 169 us -> 0 us
  waiting for transfers between devices: 408 us -> 308 us
  local copies, waits for them, and re-layouts: 20.3 us -> 92.5 us
  other arithmetic: 16.2 us -> 45.8 us
  matrix products: 51 us -> 39.2 us
    reduce_scatter x7 -> x3, waiting for transfers between devices: 343 us -> 140 us  [the longest x1 73.1 us: per_device(): lax.psum_scatter(lane_rows([expand_grad.reshape(dp_count, -1), shrink_gra...]
    all_gather x5 -> x3, waiting for transfers between devices: 36.1 us -> 168 us  [the longest x1 107 us: per_device(): lax.all_gather(jnp.concatenate([expand_weight.reshape(-1), shrink_weight....]
    unnamed x3 -> x0, blocking collectives: 101 us -> none
    all_gather x3 -> x0, blocking collectives: 67.4 us -> none  [the longest x1 29.7 us: per_device(): lax.all_gather(output_weight, 'dp', axis=1, tiled=True)]
    unnamed x14 -> x6, waiting for transfers between devices: 28.6 us -> 0.1 us
    reshape x0 -> x2, other arithmetic: none -> 21.7 us  [lane_rows(): joined = joined.reshape(joined.shape[0], -1, 128)]
    reshape x0 -> x12, local copies, waits for them, and re-layouts: none -> 16.6 us  [the longest x1 5 us: per_device(): attend_all[:, :attend_weight.size]]
    unnamed x115 -> x112, local copies, waits for them, and re-layouts: 18.6 us -> 33.3 us
  transfers between devices with their start and end apart: 13 -> 6, of which waited for: 8 -> 5; matrix products, arithmetic and copies ran while one was open for 12% -> 18% of each run, Pallas kernels for 0% -> 0%
where the time goes in v1:
time: 510 us; the launch traced here: 502 us
  waiting for transfers between devices  308 us (60%)
  local copies, waits for them, and re-layouts  92.5 us (18%)
  other arithmetic  45.8 us (9%)
  matrix products  39.2 us (8%)
  between operations  16.1 us (3%)
    all_gather x1, waiting for transfers between devices, per_device(): lax.all_gather(jnp.concatenate([expand_weight.reshape(-1), shrink_weight....  107 us
    reduce_scatter x1, waiting for transfers between devices, per_device(): lax.psum_scatter(lane_rows([expand_grad.reshape(dp_count, -1), shrink_gra...  73.1 us
    reduce_scatter x1, waiting for transfers between devices, per_device(): lax.psum_scatter(lane_rows([attend_grad.reshape(dp_count, -1), output_gra...  67.1 us
    all_gather x1, waiting for transfers between devices, per_device(): lax.all_gather(jnp.concatenate([attend_weight.reshape(-1), output_weight....  36.5 us
    unnamed x112, local copies, waits for them, and re-layouts  33.3 us
    all_gather x1, waiting for transfers between devices, per_device(): lax.all_gather(jnp.concatenate([hidden_in, cotangent, small_row], axis=0)...  23.6 us
    reshape x2, other arithmetic, lane_rows(): joined = joined.reshape(joined.shape[0], -1, 128)  21.7 us
  transfers between devices with their start and end apart: 6, of which 5 were waited for; matrix products, arithmetic and copies ran while one was open for 18% of the time, Pallas kernels for 0%

profile of v1, /device:TPU:0, one launch (start us, length us, event | category | flops | bytes accessed | tf_op | source)
XLA Modules:
  0.0 501.9 jit_solution(13771929292551655918)
XLA Ops:
  8.7 0.8 concatenate.79
  10.2 1.9 fusion.60
  12.1 1.1 copy.132
  14.3 23.6 %all-gather.11.cloned.1.call-done = bf16[4,257,1024]{2,1,0:T(8,128)(2,1)} async-done(((bf16[1,257,1024]{2,1,0:T(8,128)(2,1)}), bf16[4,257,1024]{2,1,0:T(8,128)(2,1)}) %all-gather.11.cloned.1.call-update) | async-done | bytes 2105360 | tf_op jit(solution)/shard_map/all_gather | solution.py:90
  38.8 6.8 %reshape.656 = bf16[1,1,263808]{2,1,0:T(2,128)(2,1)} reshape(bf16[263808]{0:T(1024)(128)(2,1)S(1)} %pad_maximum_fusion.2) | data formatting | bytes 1055232
  47.7 1.3 copy.176
  49.0 1.7 copy.150
  51.6 1.1 convert_reduce_fusion
  53.3 36.5 %all-gather.9.cloned.1.call-done = bf16[1048576]{0:T(1024)(128)(2,1)} async-done(((bf16[131072]{0:T(1024)(128)(2,1)}), bf16[1048576]{0:T(1024)(128)(2,1)}) %all-gather.9.cloned.1.call-update) | async-done | bytes 2097168 | tf_op jit(solution)/shard_map/all_gather | solution.py:126
  89.8 3.8 reshape.653
  93.6 2.7 slice.255
  96.2 5.0 reshape.622
  101.2 1.1 slice_bitcast_fusion.1
  103.1 0.9 copy.209
  104.0 2.0 copy.136
  106.0 2.2 fusion.47
  108.2 107.4 %all-gather.13.cloned.1.call-done = bf16[8,1,263808]{2,1,0:T(2,128)(2,1)} async-done(((bf16[1,1,263808]{2,1,0:T(2,128)(2,1)}), bf16[8,1,263808]{2,1,0:T(2,128)(2,1)}) %all-gather.13.cloned.1.call-update) | async-done | bytes 4220944 | tf_op jit(solution)/shard_map/all_gather | solution.py:98
  215.7 5.6 %copy.205 = bf16[8,1,263808]{2,0,1:T(8,128)(2,1)S(1)} copy(bf16[8,1,263808]{2,1,0:T(2,128)(2,1)} %all-gather.13.cloned.1.call-done) | data formatting | bytes 8441856
  221.2 2.3 slice_bitcast_fusion
  229.8 2.5 add_convert_fusion.4
  232.2 1.0 convolution_add_fusion
  234.1 0.9 fusion.86
  236.6 1.6 fusion.48
  238.2 1.4 multiply_reduce_fusion
  239.6 1.2 multiply_convert_fusion
  240.9 1.6 fusion.42
  242.4 1.3 fusion.43
  243.7 3.8 reshape.618
  247.5 3.2 copy.207
  250.7 3.9 copy.131
  254.7 1.8 copy.143
  256.4 1.0 slice.364
  257.5 1.0 slice.365
  258.5 1.0 subtract_convert_fusion.1
  259.5 0.8 pad_maximum_fusion.6
  260.3 1.8 copy.141
  262.1 1.8 copy.142
  263.9 8.4 %multiply_convert_fusion.1 = (bf16[512,1024]{1,0:T(8,128)(2,1)}, f32[512,1024]{1,0:T(8,128)S(1)}, f32[512,1024]{1,0:T(8,128)S(1)}) fusion(f32[1024]{0:T(1024)} %fusion.72, bf16[512,1024]{1,0:T(8,128)(2,1)} %bitcast.220, bf16[1024,1024]{1,0:T(8,128)(2,1)} %reshape.618), kind=kOutput, calls=%fused_computation.58 | convolution fusion | flops 1108344832 | bytes 8392704 | tf_op jit(solution)/shard_map/dot_general | solution.py:142
  272.3 2.1 fusion.87
  274.5 2.0 bitcast_convert_fusion
  276.6 4.5 add_convert_fusion
  282.3 3.2 fusion.88
  287.3 2.2 fusion.8
  290.3 2.5 convert_bitcast_fusion
  292.8 2.6 copy.157
  295.4 3.5 copy.206
  298.9 2.7 convolution_convert_fusion
  301.6 3.8 reshape.635
  305.4 14.6 %fusion.5 = bf16[8,2050,128]{2,0,1:T(8,128)(2,1)S(1)} fusion(bf16[8,32]{1,0:T(8,128)(2,1)S(1)} %convert_bitcast_fusion.3, bf16[8,128]{1,0:T(8,128)(2,1)S(1)} %bitcast.241, bf16[8,131072]{1,0:T(8,128)(2,1)S(1)} %bitcast.206, bf16[8,131072]{1,0:T(8,128)(2,1)} %reshape.635), kind=kLoop, calls=%fused_computation.10 | loop fusion | flops 20992000 | bytes 8395264 | tf_op jit(solution)/shard_map/reshape | solution.py:40
  320.6 2.3 pad.34.clone
  323.3 0.9 copy-done.3
  325.7 2.2 convolution_convert_fusion.1
  328.0 1.4 copy.149
  329.3 3.0 reshape.628
  333.2 7.1 %fusion.12 = bf16[8,1026,128]{2,0,1:T(8,128)(2,1)S(1)} fusion(bf16[8,96]{1,0:T(8,128)(2,1)S(1)} %reshape.631, bf16[8,128]{1,0:T(8,128)(2,1)S(1)} %reshape.632, bf16[8,32768]{1,0:T(8,128)(2,1)S(1)} %bitcast.219, bf16[8,98304]{1,0:T(8,128)(2,1)} %reshape.628), kind=kLoop, calls=%fused_computation.24 | loop fusion | flops 12607488 | bytes 4201984 | tf_op jit(solution)/shard_map/reshape | solution.py:40
  340.6 1.5 pad.32.clone
  344.1 0.9 fusion.81
  345.0 1.0 multiply_add_fusion
  346.0 73.1 %reduce-scatter.8.cloned.1.call-done = bf16[2064,128]{1,0:T(8,128)(2,1)} async-done(((bf16[16512,128]{1,0:T(8,128)(2,1)}), bf16[2064,128]{1,0:T(8,128)(2,1)}) %reduce-scatter.8.cloned.1.call-update) | async-done | bytes 528400 | tf_op jit(solution)/shard_map/reduce_scatter | solution.py:162
  419.1 1.9 slice_convert_fusion.5
  421.1 0.9 reshape.649
  422.6 67.1 %reduce-scatter.6.cloned.1.call-done = bf16[1040,128]{1,0:T(8,128)(2,1)} async-done(((bf16[8320,128]{1,0:T(8,128)(2,1)}), bf16[1040,128]{1,0:T(8,128)(2,1)}) %reduce-scatter.6.cloned.1.call-update) | async-done | bytes 266256 | tf_op jit(solution)/shard_map/reduce_scatter | solution.py:280
  489.8 1.0 slice.284
  491.0 0.8 copy.160
  (189 shorter events, 29.1 us)
Async XLA Ops:
  7.2 6.2 %copy-start.28 = (bf16[256,128]{1,0:T(8,128)(2,1)S(1)}, bf16[256,128]{1,0:T(8,128)(2,1)}, u32[]{:S(2)}) copy-start(bf16[256,128]{1,0:T(8,128)(2,1)} %param.28) | copy-start | bytes 196612
  7.2 7.0 %copy-start.26 = (bf16[128,1024]{1,0:T(8,128)(2,1)S(1)}, bf16[128,1024]{1,0:T(8,128)(2,1)}, u32[]{:S(2)}) copy-start(bf16[128,1024]{1,0:T(8,128)(2,1)} %param.30) | copy-start | bytes 786436
  7.2 31.6 %copy-start.27 = (bf16[1024,128]{1,0:T(8,128)(2,1)S(1)}, bf16[1024,128]{1,0:T(8,128)(2,1)}, u32[]{:S(2)}) copy-start(bf16[1024,128]{1,0:T(8,128)(2,1)} %param.32) | copy-start | bytes 786436
  7.2 30.7 %all-gather.11.cloned.1.call-start = ((), (), s32[]{:S(2)}) async-start(), calls=%async_computation.7 | async-start | bytes 2703360 | tf_op jit(solution)/shard_map/all_gather | solution.py:90
  12.1 77.7 %all-gather.9.cloned.1.call-start = ((), (), s32[]{:S(2)}) async-start(), calls=%async_computation.6 | async-start | bytes 2359296 | tf_op jit(solution)/shard_map/all_gather | solution.py:126
  14.2 201.5 %all-gather.13.cloned.1.call-start = ((), (), s32[]{:S(2)}) async-start(), calls=%async_computation.8 | async-start | bytes 9497088 | tf_op jit(solution)/shard_map/all_gather | solution.py:98
  14.2 32.2 %copy-start.34 = (s32[1,512]{1,0:T(1,128)S(1)}, s32[1,512]{1,0:T(1,128)}, u32[]{:S(2)}) copy-start(s32[1,512]{1,0:T(1,128)} %param.20) | copy-start | bytes 6148
  45.6 2.1 slice-start
  45.6 286.7 %reduce-scatter.4.cloned.1.call-start = ((), (), s32[]{:S(2)}) async-start(), calls=%async_computation.3 | async-start | bytes 4177920 | tf_op jit(solution)/shard_map/reduce_scatter | solution.py:265
  47.6 186.4 %copy-start.5 = (pred[512,512]{0,1:T(8,128)(4,1)}, pred[512,512]{0,1:T(8,128)(4,1)S(1)}, u32[]{:S(2)}) copy-start(pred[512,512]{0,1:T(8,128)(4,1)S(1)} %fusion.57) | copy-start | bytes 786436
  47.7 3.0 copy-start
  50.6 239.7 %copy-start.2 = (bf16[512,8,128]{0,2,1:T(8,128)(2,1)}, bf16[512,8,128]{0,2,1:T(8,128)(2,1)S(1)}, u32[]{:S(2)}) copy-start(bf16[512,8,128]{0,2,1:T(8,128)(2,1)S(1)} %copy.150) | copy-start | bytes 3145732
  51.6 42.0 %copy-start.35 = (f32[4,128]{1,0:T(4,128)}, f32[4,128]{1,0:T(4,128)S(1)}, u32[]{:S(2)}) copy-start(f32[4,128]{1,0:T(4,128)S(1)} %get-tuple-element.138) | copy-start | bytes 6148
  102.3 0.8 copy-start.12
  227.4 5.9 %copy-start.30 = (f32[1024]{0:T(1024)}, f32[1024]{0:T(1024)S(1)}, u32[]{:S(2)}) copy-start(f32[1024]{0:T(1024)S(1)} %reshape.643) | copy-start | bytes 12292
  228.2 5.1 %copy-start.32 = (f32[1024]{0:T(1024)}, f32[1024]{0:T(1024)S(1)}, u32[]{:S(2)}) copy-start(f32[1024]{0:T(1024)S(1)} %reshape.640) | copy-start | bytes 12292
  229.0 4.3 copy-start.37
  229.8 3.5 copy-start.39
  229.8 2.5 copy-start.8
  233.3 0.7 copy-start.29
  235.6 1.0 copy-start.6
  235.6 1.0 copy-start.25
  263.9 8.4 %copy-start.1 = (bf16[1,8,1024,128]{3,1,2,0:T(8,128)(2,1)S(1)}, bf16[1,8,1024,128]{3,1,2,0:T(8,128)(2,1)}, u32[]{:S(2)}) copy-start(bf16[1,8,1024,128]{3,1,2,0:T(8,128)(2,1)} %get-tuple-element.93) | copy-start | bytes 6291460
  263.9 8.4 %copy-start.41 = (f32[1024]{0:T(1024)S(1)}, f32[1024]{0:T(1024)}, u32[]{:S(2)}) copy-start(f32[1024]{0:T(1024)} %fusion.72) | copy-start | bytes 12292
  272.3 2.1 copy-start.9
  272.3 2.1 copy-start.13
  272.3 2.1 copy-start.15
  272.3 2.1 copy-start.17
  274.5 2.1 copy-start.45
  274.5 2.1 copy-start.11
  274.5 2.1 copy-start.31
  274.5 2.1 copy-start.33
  274.5 2.1 copy-start.38
  274.5 2.1 copy-start.40
  274.5 2.1 copy-start.42
  274.5 2.1 copy-start.43
  282.2 3.3 copy-start.10
  285.5 1.2 copy-start.20
  285.5 1.5 copy-start.21
  289.5 0.7 copy-start.36
  289.5 129.6 %reduce-scatter.8.cloned.1.call-start = ((), (), s32[]{:S(2)}) async-start(), calls=%async_computation.5 | async-start | bytes 4755456 | tf_op jit(solution)/shard_map/reduce_scatter | solution.py:162
  295.4 3.5 copy-start.46
  295.4 3.5 copy-start.47
  323.0 1.2 copy-start.3
  323.0 2.3 copy-start.14
  323.0 2.3 copy-start.16
  323.0 2.3 copy-start.18
  323.0 166.7 %reduce-scatter.6.cloned.1.call-start = ((), (), s32[]{:S(2)}) async-start(), calls=%async_computation.4 | async-start | bytes 2396160 | tf_op jit(solution)/shard_map/reduce_scatter | solution.py:280
  342.2 1.2 copy-start.23
  342.2 1.3 copy-start.19
  342.2 1.9 copy-start.24
  343.5 1.6 copy-start.22
  419.1 2.8 copy-start.7
  422.1 72.0 %copy-start.44 = (f32[32]{0:T(128)}, f32[32]{0:T(128)S(1)}, u32[]{:S(2)}) copy-start(f32[32]{0:T(128)S(1)} %slice.287) | copy-start | bytes 388
  489.8 2.1 copy-start.4
Sparse Core Ops, SparseCore 0:
  12.2 25.6 all-gather.10
  40.6 49.1 all-gather.8
  92.0 123.6 all-gather.12
  289.7 37.2 reduce-scatter.3
  330.5 88.5 reduce-scatter.7
  422.5 67.2 reduce-scatter.5
